TPU v7x, 512 devices: a whole 4x4x16 slice. The times are simulated.
512 devices in a mesh: grp: 16 (over z_hi, x, core), dev: 32 (over y, z_lo).
Axes of the slice: x: 4, y: 4, z: 16 (z_hi: 2, z_lo: 8; z = z_hi * 8 + z_lo), core: 2. Of those that a mesh axis runs over, the one named last changes fastest.
Arguments:
- samples: bfloat16 [16384, 1024], P(('grp', 'dev')), may hold values from -0.1875 to 0.1875
- set_labels: int32 [16384], P(('grp', 'dev')), may hold values 0 or 1
- sign_words: int32 [16384, 25], P(('grp', 'dev')), may hold values from 0 to 2097151
- corpus: bfloat16 [16384, 1024], P(('grp', 'dev')), may hold values from -0.1875 to 0.1875
- scale_grid: float32 [16], replicated, may hold values from 0.25 to 4
- scale_pick: int32 [4], replicated, may hold values from 0 to 15
Outputs:
- quad_forms: float32 [4, 512], replicated
- test_scores: float32 [4], replicated
- proof: float32 [4, 16384], P(None, ('grp', 'dev'))
Inputs may be any that keep to these rules, and one draw needn't show every extreme that they name: `sign_words`: every word is below 2 ** 21; each of its 21 bits is a sign, 1 for +1 and 0 for -1. `scale_pick`: indices into the grid, from 0 to 15.
All inputs are finite; a program needn't handle non-finite values. No bound on the sum of `set_labels` on one device may be relied on, other than what follows from the above.
Results may differ from a plain program's by a relative error of at most 0.0099.
Values may be sent and summed in bfloat16 or wider, within the bound.
No kernel may reach another device: no remote copies, remote signals or barrier semaphores. Data moves between devices by JAX's collectives and lax.ppermute only.
A program may use at most 64 MiB of HBM per device.

v0:
```python
import numpy as np
import jax
import jax.numpy as jnp
from jax import lax
from jax.sharding import PartitionSpec as P

NB = 4
BOOT = 511
D = 1024
META = 128
CHUNK = 7
word_bits = 21


def make_vectors(set_labels, sign_words):
    weights = (1 - 2 * set_labels).astype(jnp.float32)
    shifts = jnp.arange(word_bits, dtype=jnp.int32)
    bit_flags = jnp.right_shift(sign_words[:, :, None], shifts[None, None, :]) & 1
    bit_flags = bit_flags.reshape(sign_words.shape[0], -1)[:, :BOOT]
    sign_values = (2 * bit_flags - 1).astype(jnp.float32)
    vectors = jnp.concatenate([weights[:, None], sign_values * weights[:, None]], axis=1)
    return vectors.astype(jnp.bfloat16)


def band_scales(scale_grid, scale_pick):
    onehot = (
        scale_pick[:, None] == jnp.arange(scale_grid.shape[0], dtype=jnp.int32)[None, :]
    ).astype(jnp.float32)
    chosen = jnp.sum(onehot * scale_grid[None, :], axis=1)
    return 0.5 / chosen


def squares(matrix):
    wide = matrix.astype(jnp.float32)
    return jnp.sum(wide * wide, axis=1)


def distances(left, left_sq, right, right_sq):
    cross = lax.dot_general(
        left, right, (((1,), (1,)), ((), ())), preferred_element_type=jnp.float32
    )
    return left_sq[:, None] + right_sq[None, :] - 2.0 * cross


def pack_meta(set_labels, sign_words):
    words = sign_words.shape[1]
    chunks = [sign_words >> CHUNK * c & (1 << CHUNK) - 1 for c in range(3)]
    meta = jnp.concatenate([set_labels[:, None]] + chunks, axis=1)
    pad = META - meta.shape[1]
    meta = jnp.pad(meta, ((0, 0), (0, pad)))
    return (meta.astype(jnp.bfloat16), words)


def unpack(buf, words):
    rows = buf[:, :D]
    meta = buf[:, D : D + 1 + 3 * words].astype(jnp.float32).astype(jnp.int32)
    labels = meta[:, 0]
    c = [meta[:, 1 + k * words : 1 + (k + 1) * words] for k in range(3)]
    sign_words = c[0] + (c[1] << CHUNK) + (c[2] << 2 * CHUNK)
    return (rows, make_vectors(labels, sign_words))


def xor_gather(x, axis, n, bits):
    idx = lax.axis_index(axis)
    buf = x[None]
    for b in bits:
        k = 1 << b
        other = lax.ppermute(buf, axis, [(i, i ^ k) for i in range(n)])
        lo = idx & k == 0
        buf = jnp.where(lo, jnp.concatenate([buf, other]), jnp.concatenate([other, buf]))
    order = [sum(((t >> j & 1) << b for j, b in enumerate(bits))) for t in range(n)]
    return (buf, order)


def per_device(samples, set_labels, sign_words, corpus, scale_grid, scale_pick):
    scales = band_scales(scale_grid, scale_pick)
    n_grp = lax.axis_size("grp")
    n_dev = lax.axis_size("dev")
    rows_here = samples.shape[0]
    total = rows_here * n_grp * n_dev
    inv_root = jnp.float32(1.0) / jnp.sqrt(jnp.float32(total))
    meta, words = pack_meta(set_labels, sign_words)
    own = jnp.concatenate([samples, meta], axis=1)
    own_wide = jnp.concatenate([own, corpus], axis=1)
    grp_bits = [b for b in range(1, n_grp.bit_length() - 1)] + [0]
    dev_bits = list(range(n_dev.bit_length() - 1))
    col_buf, col_order = xor_gather(own_wide, "grp", n_grp, grp_bits)
    blk_buf, _ = xor_gather(own, "dev", n_dev, dev_bits)
    col_buf = col_buf.reshape(n_grp * rows_here, -1)
    blk_buf = blk_buf.reshape(n_dev * rows_here, -1)
    col_rows, col_vec = unpack(col_buf[:, : D + META], words)
    col_corpus = col_buf[:, D + META :]
    block_rows, block_vec = unpack(blk_buf, words)
    col_sq = squares(col_rows)
    block_sq = squares(block_rows)
    dist = distances(block_rows, block_sq, col_rows, col_sq)
    block_wide = block_vec.astype(jnp.float32)
    forms = []
    for kernel_id in range(NB):
        kern = jnp.exp(-dist * scales[kernel_id]).astype(jnp.bfloat16)
        product = jnp.dot(kern, col_vec, preferred_element_type=jnp.float32)
        forms.append(jnp.sum(block_wide * product, axis=0))
    forms_part = jnp.stack(forms)
    cdist = distances(col_corpus, squares(col_corpus), block_rows, block_sq)
    weights = block_vec[:, 0]
    proofs = []
    for kernel_id in range(NB):
        kern = jnp.exp(-cdist * scales[kernel_id]).astype(jnp.bfloat16)
        proofs.append(jnp.dot(kern, weights, preferred_element_type=jnp.float32))
    proof_part = jnp.stack(proofs).reshape(NB, n_grp, rows_here)
    inverse = np.argsort(np.array(col_order))
    proof_part = jnp.take(proof_part, jnp.asarray(inverse, jnp.int32), axis=1)
    proof_part = jnp.transpose(proof_part, (1, 0, 2))
    got = lax.all_to_all(proof_part, "grp", 0, 0, tiled=True)
    proof = jnp.sum(got, axis=0) * inv_root
    quad_forms = lax.psum(forms_part, ("grp", "dev")) / total
    bootstrap = quad_forms[:, 1:]
    centre = jnp.mean(bootstrap, axis=1)
    spread = jnp.mean(jnp.square(bootstrap - centre[:, None]), axis=1)
    test_scores = (quad_forms[:, 0] - centre) / jnp.sqrt(spread + 1e-06)
    return (quad_forms, test_scores, proof)


def solution(mesh):
    in_specs = (
        P(("grp", "dev"), None),
        P(("grp", "dev")),
        P(("grp", "dev"), None),
        P(("grp", "dev"), None),
        P(),
        P(),
    )
    out_specs = (P(), P(), P(None, ("grp", "dev")))
    return jax.shard_map(
        per_device, mesh=mesh, in_specs=in_specs, out_specs=out_specs, check_vma=False
    )
```

profile of v0, /device:TPU:1, one launch (start us, length us, event | category | flops | bytes accessed | tf_op | source)
XLA Modules:
  0.0 325.1 jit_solution(3288057333134248958)
XLA Ops:
  0.6 0.7 and_convert_fusion.2
  1.4 0.7 convert_bitcast_fusion
  2.0 0.1 copy.32
  2.2 0.9 maximum_bitcast_fusion
  3.1 3.9 %collective-permute-start.5 = (bf16[1,32,2176]{2,1,0:T(8,128)(2,1)S(1)}, bf16[1,32,2176]{2,1,0:T(8,128)(2,1)S(1)}, u32[]{:S(2)}, u32[]{:S(2)}) collective-permute-start(bf16[1,32,2176]{2,1,0:T(8,128)(2,1)S(1)} %maximum_bitcast_fusion), channel_id=1, source_target_pairs={{0,64},{32,96},{64,0},{96,32},{128,192},{160,224},{192,128},{224,1... | collective-permute-start | bytes 417800 | tf_op jit(solution)/shard_map/ppermute | solution.py:68
  7.1 2.4 collective-permute-done.5
  9.5 5.5 %collective-permute-start.6 = (bf16[2,32,2176]{2,1,0:T(8,128)(2,1)S(1)}, bf16[2,32,2176]{2,1,0:T(8,128)(2,1)S(1)}, u32[]{:S(2)}, u32[]{:S(2)}) collective-permute-start(bf16[2,32,2176]{2,1,0:T(8,128)(2,1)S(1)} %maximum_select_fusion.7), channel_id=1, source_target_pairs={{0,128},{32,160},{64,192},{96,224},{128,0},{160,32},{192,64},{224,... | collective-permute-start | bytes 835592 | tf_op jit(solution)/shard_map/ppermute | solution.py:68
  15.1 0.8 maximum_bitcast_fusion.1
  15.9 3.5 %collective-permute-start = (bf16[1,32,1152]{2,1,0:T(8,128)(2,1)S(1)}, bf16[1,32,1152]{2,1,0:T(8,128)(2,1)S(1)}, u32[]{:S(2)}, u32[]{:S(2)}) collective-permute-start(bf16[1,32,1152]{2,1,0:T(8,128)(2,1)S(1)} %maximum_bitcast_fusion.1), channel_id=1, source_target_pairs={{0,1},{1,0},{2,3},{3,2},{4,5},{5,4},{6,7},{7,6},{8,9},{9,8},{10,11... | collective-permute-start | bytes 221192 | tf_op jit(solution)/shard_map/ppermute | solution.py:68
  19.5 0.1 maximum_select_fusion.5
  19.6 16.4 %collective-permute-start.7 = (bf16[4,32,2176]{2,1,0:T(8,128)(2,1)S(1)}, bf16[4,32,2176]{2,1,0:T(8,128)(2,1)S(1)}, u32[]{:S(2)}, u32[]{:S(2)}) collective-permute-start(bf16[4,32,2176]{2,1,0:T(8,128)(2,1)S(1)} %maximum_select_fusion.5), channel_id=1, source_target_pairs={{0,256},{32,288},{64,320},{96,352},{128,384},{160,416},{192,448},{... | collective-permute-start | bytes 1671176 | tf_op jit(solution)/shard_map/ppermute | solution.py:68
  36.1 3.2 collective-permute-start.1
  39.4 52.6 %collective-permute-done.1 = bf16[2,32,1152]{2,1,0:T(8,128)(2,1)S(1)} collective-permute-done((bf16[2,32,1152]{2,1,0:T(8,128)(2,1)S(1)}, bf16[2,32,1152]{2,1,0:T(8,128)(2,1)S(1)}, u32[]{:S(2)}, u32[]{:S(2)}) %collective-permute-start.1) | collective-permute-done | bytes 147488 | tf_op jit(solution)/shard_map/ppermute | solution.py:68
  92.1 2.0 collective-permute-start.2
  94.1 0.2 maximum_select_fusion.3
  94.3 2.7 collective-permute-start.8
  97.0 26.5 %collective-permute-done.2 = bf16[4,32,1152]{2,1,0:T(8,128)(2,1)S(1)} collective-permute-done((bf16[4,32,1152]{2,1,0:T(8,128)(2,1)S(1)}, bf16[4,32,1152]{2,1,0:T(8,128)(2,1)S(1)}, u32[]{:S(2)}, u32[]{:S(2)}) %collective-permute-start.2) | collective-permute-done | bytes 294944 | tf_op jit(solution)/shard_map/ppermute | solution.py:68
  123.5 0.1 maximum_select_fusion.4
  123.6 3.2 collective-permute-start.3
  126.8 0.1 shift_right_arithmetic.67
  127.0 0.2 select_reduce_fusion
  127.2 0.7 fusion.55
  127.8 12.1 %collective-permute-done.3 = bf16[8,32,1152]{2,1,0:T(8,128)(2,1)S(1)} collective-permute-done((bf16[8,32,1152]{2,1,0:T(8,128)(2,1)S(1)}, bf16[8,32,1152]{2,1,0:T(8,128)(2,1)S(1)}, u32[]{:S(2)}, u32[]{:S(2)}) %collective-permute-start.3) | collective-permute-done | bytes 589856 | tf_op jit(solution)/shard_map/ppermute | solution.py:68
  139.9 1.2 maximum_select_fusion.2
  141.1 4.8 %collective-permute-start.4 = (bf16[16,32,1152]{2,1,0:T(8,128)(2,1)}, bf16[16,32,1152]{2,1,0:T(8,128)(2,1)}, u32[]{:S(2)}, u32[]{:S(2)}) collective-permute-start(bf16[16,32,1152]{2,1,0:T(8,128)(2,1)} %maximum_select_fusion.2), channel_id=1, source_target_pairs={{0,16},{1,17},{2,18},{3,19},{4,20},{5,21},{6,22},{7,23},{8,24},{9,... | collective-permute-start | bytes 3538952 | tf_op jit(solution)/shard_map/ppermute | solution.py:68
  145.9 2.0 maximum_select_fusion.1
  147.9 0.1 copy.48
  148.0 0.9 convert_convert_fusion.1
  148.9 1.0 fusion.26
  149.9 0.1 shift_right_arithmetic.70
  150.1 1.2 shift_right_arithmetic.71
  151.2 0.8 fusion.53
  152.0 0.5 multiply_reduce_fusion.1
  152.5 0.3 fusion.17
  152.8 18.2 %collective-permute-done.4 = bf16[16,32,1152]{2,1,0:T(8,128)(2,1)} collective-permute-done((bf16[16,32,1152]{2,1,0:T(8,128)(2,1)}, bf16[16,32,1152]{2,1,0:T(8,128)(2,1)}, u32[]{:S(2)}, u32[]{:S(2)}) %collective-permute-start.4) | collective-permute-done | bytes 1179680 | tf_op jit(solution)/shard_map/ppermute | solution.py:68
  171.0 2.6 maximum_select_fusion
  173.6 0.5 multiply_reduce_fusion
  174.1 0.9 copy-done
  175.0 0.2 copy.47
  175.3 0.3 shift_right_arithmetic.64
  175.6 1.7 shift_right_arithmetic.65
  177.3 2.2 fusion.9
  179.6 2.5 subtract_negate_fusion.1
  182.1 1.6 fusion
  183.7 1.6 fusion.1
  185.4 1.6 fusion.2
  186.9 1.6 fusion.3
  188.5 102.5 %psum.7 = f32[4,512]{1,0:T(4,128)S(1)} all-reduce(f32[4,512]{1,0:T(4,128)S(1)} %pad_maximum_fusion.3), channel_id=1, replica_groups=mesh['grp'=16,'dev'=32] {'grp','dev'}, use_global_device_ids=true, to_apply=%region_7.8 | all-reduce | flops 2048 | bytes 16384 | tf_op jit(solution)/shard_map/psum | solution.py:116
  291.1 0.2 slice_reduce_fusion
  291.2 0.1 slice_reduce_fusion.1
  291.4 6.0 %exponential_convert_fusion.3 = (bf16[512,1024]{1,0:T(8,128)(2,1)S(1)}, bf16[512,1024]{1,0:T(8,128)(2,1)S(1)}, bf16[512,1024]{1,0:T(8,128)(2,1)S(1)}, bf16[512,1024]{1,0:T(8,128)(2,1)S(1)}) fusion(f32[]{:T(128)} %bitcast.6, f32[]{:T(128)} %bitcast.13, f32[]{:T(128)} %bitcast.11, f32[]{:T(128)} %bitcast.9, bf16[1024,1152]{1,0:T(8,128)(2,1)S(1)} %bitcast.50, ...), kind=kOutput, calls=%fused_computation.22 | convolution fusion | flops 1080033280 | bytes 7348224 | tf_op jit(solution)/shard_map/dot_general | solution.py:39
  297.4 0.8 fusion.43
  298.1 0.8 fusion.41
  298.9 0.8 fusion.39
  299.7 0.8 fusion.37
  300.6 0.6 gather_fusion
  301.2 0.7 reshape.96
  301.8 7.2 %all-to-all-start = ((f32[16,1,128]{2,1,0:T(1,128)}), f32[16,1,128]{2,1,0:T(1,128)S(1)}, u32[]{:S(2)}, u32[]{:S(2)}) async-start(f32[16,1,128]{2,1,0:T(1,128)} %reshape.96), calls=%async_computation | async-start | bytes 16384 | tf_op jit(solution)/shard_map/all_to_all | solution.py:114
  309.0 0.2 multiply_reduce_fusion.3
  309.2 0.5 rsqrt_multiply_fusion
  309.8 13.5 %all-to-all-done = f32[16,1,128]{2,1,0:T(1,128)S(1)} async-done(((f32[16,1,128]{2,1,0:T(1,128)}), f32[16,1,128]{2,1,0:T(1,128)S(1)}, u32[]{:S(2)}, u32[]{:S(2)}) %all-to-all-start) | async-done | bytes 8224 | tf_op jit(solution)/shard_map/all_to_all | solution.py:114
  323.3 0.5 broadcast.108
  323.8 0.7 reduce.2
  324.6 0.6 broadcast_multiply_fusion.1
  (38 shorter events, 0.6 us)
Async XLA Ops:
  3.1 6.4 %collective-permute-start.5 = (bf16[1,32,2176]{2,1,0:T(8,128)(2,1)S(1)}, bf16[1,32,2176]{2,1,0:T(8,128)(2,1)S(1)}, u32[]{:S(2)}, u32[]{:S(2)}) collective-permute-start(bf16[1,32,2176]{2,1,0:T(8,128)(2,1)S(1)} %maximum_bitcast_fusion), channel_id=1, source_target_pairs={{0,64},{32,96},{64,0},{96,32},{128,192},{160,224},{192,128},{224,1... | collective-permute-start | bytes 417800 | tf_op jit(solution)/shard_map/ppermute | solution.py:68
  9.5 10.0 %collective-permute-start.6 = (bf16[2,32,2176]{2,1,0:T(8,128)(2,1)S(1)}, bf16[2,32,2176]{2,1,0:T(8,128)(2,1)S(1)}, u32[]{:S(2)}, u32[]{:S(2)}) collective-permute-start(bf16[2,32,2176]{2,1,0:T(8,128)(2,1)S(1)} %maximum_select_fusion.7), channel_id=1, source_target_pairs={{0,128},{32,160},{64,192},{96,224},{128,0},{160,32},{192,64},{224,... | collective-permute-start | bytes 835592 | tf_op jit(solution)/shard_map/ppermute | solution.py:68
  15.9 20.1 %collective-permute-start = (bf16[1,32,1152]{2,1,0:T(8,128)(2,1)S(1)}, bf16[1,32,1152]{2,1,0:T(8,128)(2,1)S(1)}, u32[]{:S(2)}, u32[]{:S(2)}) collective-permute-start(bf16[1,32,1152]{2,1,0:T(8,128)(2,1)S(1)} %maximum_bitcast_fusion.1), channel_id=1, source_target_pairs={{0,1},{1,0},{2,3},{3,2},{4,5},{5,4},{6,7},{7,6},{8,9},{9,8},{10,11... | collective-permute-start | bytes 221192 | tf_op jit(solution)/shard_map/ppermute | solution.py:68
  19.6 74.5 %collective-permute-start.7 = (bf16[4,32,2176]{2,1,0:T(8,128)(2,1)S(1)}, bf16[4,32,2176]{2,1,0:T(8,128)(2,1)S(1)}, u32[]{:S(2)}, u32[]{:S(2)}) collective-permute-start(bf16[4,32,2176]{2,1,0:T(8,128)(2,1)S(1)} %maximum_select_fusion.5), channel_id=1, source_target_pairs={{0,256},{32,288},{64,320},{96,352},{128,384},{160,416},{192,448},{... | collective-permute-start | bytes 1671176 | tf_op jit(solution)/shard_map/ppermute | solution.py:68
  36.1 90.8 %copy-start.5 = (s32[16]{0:T(128)S(1)}, s32[16]{0:T(128)}, u32[]{:S(2)}) copy-start(s32[16]{0:T(128)} %constant.97) | copy-start | bytes 196
  36.1 90.8 %copy-start.6 = (f32[16]{0:T(128)S(1)}, f32[16]{0:T(128)}, u32[]{:S(2)}) copy-start(f32[16]{0:T(128)} %param.11) | copy-start | bytes 196
  36.1 90.8 %copy-start.7 = (s32[4]{0:T(128)S(1)}, s32[4]{0:T(128)}, u32[]{:S(2)}) copy-start(s32[4]{0:T(128)} %param.12) | copy-start | bytes 52
  36.1 55.9 %collective-permute-start.1 = (bf16[2,32,1152]{2,1,0:T(8,128)(2,1)S(1)}, bf16[2,32,1152]{2,1,0:T(8,128)(2,1)S(1)}, u32[]{:S(2)}, u32[]{:S(2)}) collective-permute-start(bf16[2,32,1152]{2,1,0:T(8,128)(2,1)S(1)} %maximum_select_fusion.8), channel_id=1, source_target_pairs={{0,2},{1,3},{2,0},{3,1},{4,6},{5,7},{6,4},{7,5},{8,10},{9,11},{10,... | collective-permute-start | bytes 442376 | tf_op jit(solution)/shard_map/ppermute | solution.py:68
  92.1 31.4 %collective-permute-start.2 = (bf16[4,32,1152]{2,1,0:T(8,128)(2,1)S(1)}, bf16[4,32,1152]{2,1,0:T(8,128)(2,1)S(1)}, u32[]{:S(2)}, u32[]{:S(2)}) collective-permute-start(bf16[4,32,1152]{2,1,0:T(8,128)(2,1)S(1)} %maximum_select_fusion.6), channel_id=1, source_target_pairs={{0,4},{1,5},{2,6},{3,7},{4,0},{5,1},{6,2},{7,3},{8,12},{9,13},{10,... | collective-permute-start | bytes 884744 | tf_op jit(solution)/shard_map/ppermute | solution.py:68
  94.3 51.6 %collective-permute-start.8 = (bf16[8,32,2176]{2,1,0:T(8,128)(2,1)S(1)}, bf16[8,32,2176]{2,1,0:T(8,128)(2,1)}, u32[]{:S(2)}, u32[]{:S(2)}) collective-permute-start(bf16[8,32,2176]{2,1,0:T(8,128)(2,1)S(1)} %maximum_select_fusion.3), channel_id=1, source_target_pairs={{0,32},{32,0},{64,96},{96,64},{128,160},{160,128},{192,224},{224,1... | collective-permute-start | bytes 3342344 | tf_op jit(solution)/shard_map/ppermute | solution.py:68
  123.6 16.3 %collective-permute-start.3 = (bf16[8,32,1152]{2,1,0:T(8,128)(2,1)S(1)}, bf16[8,32,1152]{2,1,0:T(8,128)(2,1)S(1)}, u32[]{:S(2)}, u32[]{:S(2)}) collective-permute-start(bf16[8,32,1152]{2,1,0:T(8,128)(2,1)S(1)} %maximum_select_fusion.4), channel_id=1, source_target_pairs={{0,8},{1,9},{2,10},{3,11},{4,12},{5,13},{6,14},{7,15},{8,0},{9,1},... | collective-permute-start | bytes 1769480 | tf_op jit(solution)/shard_map/ppermute | solution.py:68
  141.1 29.9 %collective-permute-start.4 = (bf16[16,32,1152]{2,1,0:T(8,128)(2,1)}, bf16[16,32,1152]{2,1,0:T(8,128)(2,1)}, u32[]{:S(2)}, u32[]{:S(2)}) collective-permute-start(bf16[16,32,1152]{2,1,0:T(8,128)(2,1)} %maximum_select_fusion.2), channel_id=1, source_target_pairs={{0,16},{1,17},{2,18},{3,19},{4,20},{5,21},{6,22},{7,23},{8,24},{9,... | collective-permute-start | bytes 3538952 | tf_op jit(solution)/shard_map/ppermute | solution.py:68
  147.9 4.1 %copy-start.2 = (bf16[16,32,2176]{2,1,0:T(8,128)(2,1)}, bf16[16,32,2176]{2,1,0:T(8,128)(2,1)S(1)}, u32[]{:S(2)}) copy-start(bf16[16,32,2176]{2,1,0:T(8,128)(2,1)S(1)} %maximum_select_fusion.1) | copy-start | bytes 6684676
  151.2 1.3 copy-start.3
  173.6 1.4 copy-start
  177.3 2.3 copy-start.1
  291.1 18.0 %copy-start.4 = (f32[4,512]{1,0:T(4,128)}, f32[4,512]{1,0:T(4,128)S(1)}, u32[]{:S(2)}) copy-start(f32[4,512]{1,0:T(4,128)S(1)} %broadcast_multiply_fusion) | copy-start | bytes 24580
  301.8 21.4 %all-to-all-start = ((f32[16,1,128]{2,1,0:T(1,128)}), f32[16,1,128]{2,1,0:T(1,128)S(1)}, u32[]{:S(2)}, u32[]{:S(2)}) async-start(f32[16,1,128]{2,1,0:T(1,128)} %reshape.96), calls=%async_computation | async-start | bytes 16384 | tf_op jit(solution)/shard_map/all_to_all | solution.py:114
where the time goes:
time: 326 us; the launch traced here: 325 us
  waiting for transfers between devices  125 us (38%)
  blocking collectives  103 us (32%)
  starting transfers between devices  52.6 us (16%)
  other arithmetic  18.2 us (6%)
  matrix products  18.1 us (6%)
  local copies, waits for them, and re-layouts  7.41 us (2%)
    ppermute x9, waiting for transfers between devices, xor_gather(): other = lax.ppermute(buf, axis, [(i, i ^ k) for i in range(n)])  112 us
    psum x1, blocking collectives, per_device(): quad_forms = lax.psum(forms_part, ('grp', 'dev')) / total  103 us
    ppermute x9, starting transfers between devices, xor_gather(): other = lax.ppermute(buf, axis, [(i, i ^ k) for i in range(n)])  45.4 us
    all_to_all x1, waiting for transfers between devices, per_device(): got = lax.all_to_all(proof_part, 'grp', 0, 0, tiled=True)  13.5 us
    dot_general x2, matrix products, distances(): lax.dot_general(left, right, (((1,), (1,)), ((), ())), preferred_element_...  8.49 us
    all_to_all x1, starting transfers between devices, per_device(): got = lax.all_to_all(proof_part, 'grp', 0, 0, tiled=True)  7.18 us
  transfers between devices with their start and end apart: 10, of which 6 were waited for; matrix products, arithmetic and copies ran while one was open for 3% of the time, Pallas kernels for 0%

commit v1 on v0

--- a/solution.py
+++ b/solution.py
@@ -113,7 +113,8 @@
     proof_part = jnp.transpose(proof_part, (1, 0, 2))
     got = lax.all_to_all(proof_part, "grp", 0, 0, tiled=True)
     proof = jnp.sum(got, axis=0) * inv_root
-    quad_forms = lax.psum(forms_part, ("grp", "dev")) / total
+    mark_the_ladders = lambda chunk: jnp.sum(lax.all_gather(chunk, ("grp", "dev")), 0)
+    quad_forms = mark_the_ladders(forms_part) / total
     bootstrap = quad_forms[:, 1:]
     centre = jnp.mean(bootstrap, axis=1)
     spread = jnp.mean(jnp.square(bootstrap - centre[:, None]), axis=1)

time: 326 us -> 1640 us (5.03)
  waiting for transfers between devices: 125 us -> 1500 us
  blocking collectives: 103 us -> 22.1 us
    all_gather x0 -> x1, waiting for transfers between devices: none -> 1390 us  [per_device(): lax.all_gather(chunk, ('grp', 'dev'))]
    psum x1 -> x0, blocking collectives: 103 us -> none  [per_device(): quad_forms = lax.psum(forms_part, ('grp', 'dev')) / total]
    all_to_all x0 -> x1, blocking collectives: none -> 22.1 us  [per_device(): got = lax.all_to_all(proof_part, 'grp', 0, 0, tiled=True)]
  transfers between devices with their start and end apart: 10 -> 10, of which waited for: 6 -> 6; matrix products, arithmetic and copies ran while one was open for 3% -> 1% of each run, Pallas kernels for 0% -> 0%
where the time goes in v1:
time: 1640 us; the launch traced here: 1630 us
  waiting for transfers between devices  1500 us (91%)
  starting transfers between devices  45.3 us (3%)
  blocking collectives  22.1 us (1%)
  other arithmetic  21.7 us (1%)
  matrix products  18.1 us (1%)
    all_gather x1, waiting for transfers between devices, per_device(): lax.all_gather(chunk, ('grp', 'dev'))  1390 us
    ppermute x9, waiting for transfers between devices, xor_gather(): other = lax.ppermute(buf, axis, [(i, i ^ k) for i in range(n)])  112 us
    ppermute x9, starting transfers between devices, xor_gather(): other = lax.ppermute(buf, axis, [(i, i ^ k) for i in range(n)])  45.3 us
  transfers between devices with their start and end apart: 10, of which 6 were waited for; matrix products, arithmetic and copies ran while one was open for 1% of the time, Pallas kernels for 0%

profile of v1, /device:TPU:1, one launch (start us, length us, event | category | flops | bytes accessed | tf_op | source)
XLA Modules:
  0.0 1631.3 jit_solution(5167243469616031819)
XLA Ops:
  7.2 0.7 and_convert_fusion.2
  7.9 0.7 convert_bitcast_fusion
  8.6 0.1 copy.37
  8.8 0.9 maximum_bitcast_fusion
  9.7 3.9 collective-permute-start.5
  13.6 2.4 collective-permute-done.5
  16.1 5.5 collective-permute-start.6
  21.6 0.8 maximum_bitcast_fusion.1
  22.5 3.5 collective-permute-start
  26.1 0.1 maximum_select_fusion.5
  26.2 16.4 %collective-permute-start.7 = (bf16[4,32,2176]{2,1,0:T(8,128)(2,1)S(1)}, bf16[4,32,2176]{2,1,0:T(8,128)(2,1)S(1)}, u32[]{:S(2)}, u32[]{:S(2)}) collective-permute-start(bf16[4,32,2176]{2,1,0:T(8,128)(2,1)S(1)} %maximum_select_fusion.5), channel_id=1, source_target_pairs={{0,256},{32,288},{64,320},{96,352},{128,384},{160,416},{192,448},{... | collective-permute-start | bytes 1671176 | tf_op jit(solution)/shard_map/ppermute | solution.py:68
  42.7 3.1 collective-permute-start.1
  45.8 52.8 %collective-permute-done.1 = bf16[2,32,1152]{2,1,0:T(8,128)(2,1)S(1)} collective-permute-done((bf16[2,32,1152]{2,1,0:T(8,128)(2,1)S(1)}, bf16[2,32,1152]{2,1,0:T(8,128)(2,1)S(1)}, u32[]{:S(2)}, u32[]{:S(2)}) %collective-permute-start.1) | collective-permute-done | bytes 147488 | tf_op jit(solution)/shard_map/ppermute | solution.py:68
  98.6 2.0 collective-permute-start.2
  100.7 0.2 maximum_select_fusion.3
  100.9 2.7 collective-permute-start.8
  103.6 26.5 %collective-permute-done.2 = bf16[4,32,1152]{2,1,0:T(8,128)(2,1)S(1)} collective-permute-done((bf16[4,32,1152]{2,1,0:T(8,128)(2,1)S(1)}, bf16[4,32,1152]{2,1,0:T(8,128)(2,1)S(1)}, u32[]{:S(2)}, u32[]{:S(2)}) %collective-permute-start.2) | collective-permute-done | bytes 294944 | tf_op jit(solution)/shard_map/ppermute | solution.py:68
  130.1 0.1 maximum_select_fusion.4
  130.2 3.2 collective-permute-start.3
  133.5 0.2 select_reduce_fusion
  133.7 0.7 fusion.55
  134.4 12.1 collective-permute-done.3
  146.5 1.2 maximum_select_fusion.2
  147.7 4.8 collective-permute-start.4
  152.5 2.0 maximum_select_fusion.1
  154.5 0.1 copy.53
  154.6 0.9 convert_convert_fusion.1
  155.5 1.0 fusion.26
  156.5 0.1 shift_right_arithmetic.70
  156.6 1.2 shift_right_arithmetic.71
  157.8 0.8 fusion.53
  158.6 0.5 multiply_reduce_fusion.1
  159.1 0.3 fusion.17
  159.4 18.2 %collective-permute-done.4 = bf16[16,32,1152]{2,1,0:T(8,128)(2,1)} collective-permute-done((bf16[16,32,1152]{2,1,0:T(8,128)(2,1)}, bf16[16,32,1152]{2,1,0:T(8,128)(2,1)}, u32[]{:S(2)}, u32[]{:S(2)}) %collective-permute-start.4) | collective-permute-done | bytes 1179680 | tf_op jit(solution)/shard_map/ppermute | solution.py:68
  177.6 2.6 maximum_select_fusion
  180.2 0.5 multiply_reduce_fusion
  180.7 0.9 copy-done
  181.6 0.2 copy.52
  181.9 0.3 shift_right_arithmetic.64
  182.2 1.7 shift_right_arithmetic.65
  183.9 2.2 fusion.9
  186.1 2.5 subtract_negate_fusion.1
  188.7 1.6 fusion
  190.3 1.5 fusion.1
  191.8 1.7 fusion.2
  193.5 1.6 fusion.3
  195.1 0.6 maximum_bitcast_fusion.2
  195.8 6.0 exponential_convert_fusion.3
  201.8 0.8 fusion.43
  202.6 0.8 fusion.41
  203.3 0.8 fusion.39
  204.1 0.8 fusion.37
  205.0 0.6 gather_fusion
  205.6 0.1 reshape.100
  205.7 22.1 %all_to_all.5 = f32[16,1,128]{2,1,0:T(1,128)S(1)} all-to-all(f32[16,1,128]{2,1,0:T(1,128)S(1)} %reshape.100), channel_id=1, replica_groups=mesh['grp'=16,'dev'=32] {'grp'}, dimensions={0} | all-to-all | bytes 16384 | tf_op jit(solution)/shard_map/all_to_all | solution.py:114
  227.8 0.5 broadcast.108
  228.3 0.7 reduce.3
  229.1 0.6 broadcast_multiply_fusion.1
  229.7 1390.9 %all-gather.4.cloned.1.call-done = f32[512,4,512]{2,1,0:T(4,128)} async-done(((f32[1,4,512]{2,1,0:T(4,128)}), f32[512,4,512]{2,1,0:T(4,128)}) %all-gather.4.cloned.1.call-update) | async-done | bytes 4194320 | tf_op jit(solution)/shard_map/all_gather | solution.py:116
  1620.6 2.8 reduce_sum.115
  1623.4 0.2 slice_reduce_fusion
  1623.6 0.1 slice_reduce_fusion.1
  1623.7 0.2 multiply_reduce_fusion.3
  1623.9 0.5 rsqrt_multiply_fusion
  (40 shorter events, 0.7 us)
Async XLA Ops:
  7.2 1613.4 %all-gather.4.cloned.1.call-start = ((), (), s32[]{:S(2)}) async-start(), calls=%async_computation.1 | async-start | bytes 4202496 | tf_op jit(solution)/shard_map/all_gather | solution.py:116
  9.7 6.4 collective-permute-start.5
  16.1 10.0 collective-permute-start.6
  22.5 20.1 %collective-permute-start = (bf16[1,32,1152]{2,1,0:T(8,128)(2,1)S(1)}, bf16[1,32,1152]{2,1,0:T(8,128)(2,1)S(1)}, u32[]{:S(2)}, u32[]{:S(2)}) collective-permute-start(bf16[1,32,1152]{2,1,0:T(8,128)(2,1)S(1)} %maximum_bitcast_fusion.1), channel_id=1, source_target_pairs={{0,1},{1,0},{2,3},{3,2},{4,5},{5,4},{6,7},{7,6},{8,9},{9,8},{10,11... | collective-permute-start | bytes 221192 | tf_op jit(solution)/shard_map/ppermute | solution.py:68
  26.2 74.5 %collective-permute-start.7 = (bf16[4,32,2176]{2,1,0:T(8,128)(2,1)S(1)}, bf16[4,32,2176]{2,1,0:T(8,128)(2,1)S(1)}, u32[]{:S(2)}, u32[]{:S(2)}) collective-permute-start(bf16[4,32,2176]{2,1,0:T(8,128)(2,1)S(1)} %maximum_select_fusion.5), channel_id=1, source_target_pairs={{0,256},{32,288},{64,320},{96,352},{128,384},{160,416},{192,448},{... | collective-permute-start | bytes 1671176 | tf_op jit(solution)/shard_map/ppermute | solution.py:68
  42.7 90.8 %copy-start.6 = (f32[16]{0:T(128)S(1)}, f32[16]{0:T(128)}, u32[]{:S(2)}) copy-start(f32[16]{0:T(128)} %param.11) | copy-start | bytes 196
  42.7 90.8 %copy-start.7 = (s32[4]{0:T(128)S(1)}, s32[4]{0:T(128)}, u32[]{:S(2)}) copy-start(s32[4]{0:T(128)} %param.12) | copy-start | bytes 52
  42.7 55.9 %collective-permute-start.1 = (bf16[2,32,1152]{2,1,0:T(8,128)(2,1)S(1)}, bf16[2,32,1152]{2,1,0:T(8,128)(2,1)S(1)}, u32[]{:S(2)}, u32[]{:S(2)}) collective-permute-start(bf16[2,32,1152]{2,1,0:T(8,128)(2,1)S(1)} %maximum_select_fusion.8), channel_id=1, source_target_pairs={{0,2},{1,3},{2,0},{3,1},{4,6},{5,7},{6,4},{7,5},{8,10},{9,11},{10,... | collective-permute-start | bytes 442376 | tf_op jit(solution)/shard_map/ppermute | solution.py:68
  98.6 31.4 %collective-permute-start.2 = (bf16[4,32,1152]{2,1,0:T(8,128)(2,1)S(1)}, bf16[4,32,1152]{2,1,0:T(8,128)(2,1)S(1)}, u32[]{:S(2)}, u32[]{:S(2)}) collective-permute-start(bf16[4,32,1152]{2,1,0:T(8,128)(2,1)S(1)} %maximum_select_fusion.6), channel_id=1, source_target_pairs={{0,4},{1,5},{2,6},{3,7},{4,0},{5,1},{6,2},{7,3},{8,12},{9,13},{10,... | collective-permute-start | bytes 884744 | tf_op jit(solution)/shard_map/ppermute | solution.py:68
  100.9 51.6 %collective-permute-start.8 = (bf16[8,32,2176]{2,1,0:T(8,128)(2,1)S(1)}, bf16[8,32,2176]{2,1,0:T(8,128)(2,1)}, u32[]{:S(2)}, u32[]{:S(2)}) collective-permute-start(bf16[8,32,2176]{2,1,0:T(8,128)(2,1)S(1)} %maximum_select_fusion.3), channel_id=1, source_target_pairs={{0,32},{32,0},{64,96},{96,64},{128,160},{160,128},{192,224},{224,1... | collective-permute-start | bytes 3342344 | tf_op jit(solution)/shard_map/ppermute | solution.py:68
  130.2 16.3 collective-permute-start.3
  147.7 29.9 %collective-permute-start.4 = (bf16[16,32,1152]{2,1,0:T(8,128)(2,1)}, bf16[16,32,1152]{2,1,0:T(8,128)(2,1)}, u32[]{:S(2)}, u32[]{:S(2)}) collective-permute-start(bf16[16,32,1152]{2,1,0:T(8,128)(2,1)} %maximum_select_fusion.2), channel_id=1, source_target_pairs={{0,16},{1,17},{2,18},{3,19},{4,20},{5,21},{6,22},{7,23},{8,24},{9,... | collective-permute-start | bytes 3538952 | tf_op jit(solution)/shard_map/ppermute | solution.py:68
  154.5 4.1 copy-start.2
  157.8 1.3 copy-start.3
  180.2 1.4 copy-start
  183.8 2.3 copy-start.1
  193.5 2.3 copy-start.5
  1623.4 1.0 copy-start.4
Sparse Core Ops, SparseCore 0:
  195.9 1424.6 all-gather.3
